TPU v7x, 256 devices: a whole 4x4x8 slice. The times are simulated.
256 devices in a mesh: req: 8 (over x, z_hi), blk: 32 (over y, z_lo, core).
Axes of the slice: x: 4, y: 4, z: 8 (z_hi: 2, z_lo: 4; z = z_hi * 4 + z_lo), core: 2. Of those that a mesh axis runs over, the one named last changes fastest.
Arguments:
- tokens: bfloat16 [256, 128, 1536], P(('req', 'blk')), may hold values from -6 to 6
- cache_kv: bfloat16 [256, 2, 256, 384], P(('req', 'blk')), may hold values from -200 to 200
- cache_len: int32 [256], P(('req', 'blk')), may hold values from 2 to 256, as said below
- holder: int32 [256], P(('req', 'blk')), may hold values from 0 to 7, as said below
- accept: int32 [256, 128], P(('req', 'blk')), may hold values from 0 to 1, as said below
- attn_gain: float32 [1536], replicated, may hold values from 0.1 to 1.9
- q_weight: bfloat16 [1536, 768], replicated, may hold values from -0.15625 to 0.15625
- k_weight: bfloat16 [1536, 384], replicated, may hold values from -0.15625 to 0.15625
- v_weight: bfloat16 [1536, 384], replicated, may hold values from -0.15625 to 0.15625
- o_weight: bfloat16 [768, 1536], replicated, may hold values from -0.21875 to 0.21875
- ffn_gain: float32 [1536], replicated, may hold values from 0.4 to 2.5
- w_gate: bfloat16 [1536, 4096], P(None, 'blk'), may hold values from -0.15625 to 0.15625
- w_up: bfloat16 [1536, 4096], P(None, 'blk'), may hold values from -0.15625 to 0.15625
- w_down: bfloat16 [4096, 1536], P('blk'), may hold values from -0.09375 to 0.09375
Outputs:
- refined: float32 [256, 128, 1536], P(('req', 'blk'))
Inputs may be any that keep to these rules, and one draw needn't show every extreme that they name: `holder`: requests whose numbers agree modulo 32 have distinct holders. `cache_len`: some request has exactly 256 cached positions. `accept`: each request accepts exactly 64 positions.
All inputs are finite; a program needn't handle non-finite values.
Results may differ from a plain program's by a relative error of at most 0.04.
Values may be sent and summed in bfloat16 or wider, within the bound.
No kernel may reach another device: no remote copies, remote signals or barrier semaphores. Data moves between devices by JAX's collectives and lax.ppermute only.
A program may use at most 128 MiB of HBM per device.

v0:
```python
import jax
import jax.numpy as jnp
from jax import lax
from jax.sharding import PartitionSpec as P

HEAD = 96
norm_eps = 1e-05
rope_base = 100000.0


def rms_scale(values, gain_row):
    return (
        values * lax.rsqrt(jnp.mean(values * values, axis=-1, keepdims=True) + norm_eps) * gain_row
    )


def rotate_heads(flat, positions, head_count):
    half_dim = HEAD // 2
    shaped = flat.reshape(flat.shape[0], head_count, HEAD)
    freqs = jnp.exp(-jnp.log(rope_base) * 2.0 * jnp.arange(half_dim, dtype=jnp.float32) / HEAD)
    angles = positions[:, None] * freqs[None, :]
    cosine = jnp.cos(angles)[:, None, :]
    sine = jnp.sin(angles)[:, None, :]
    first_half = shaped[..., :half_dim]
    second_half = shaped[..., half_dim:]
    turned = jnp.concatenate(
        [first_half * cosine - second_half * sine, second_half * cosine + first_half * sine],
        axis=-1,
    )
    return turned.reshape(flat.shape[0], head_count * HEAD)


def attend_block(
    tok_rows,
    cache_keys,
    cache_vals,
    cache_length,
    attn_gain,
    q_weight,
    k_weight,
    v_weight,
    o_weight,
):
    block_len = tok_rows.shape[0]
    slot_len = cache_keys.shape[0]
    kv_count = k_weight.shape[1] // HEAD
    q_count = q_weight.shape[1] // HEAD
    widened = tok_rows.astype(jnp.float32)
    normed = rms_scale(widened, attn_gain).astype(jnp.bfloat16)
    positions = (cache_length + jnp.arange(block_len, dtype=jnp.int32)).astype(jnp.float32)
    queries = rotate_heads(
        jnp.dot(normed, q_weight, preferred_element_type=jnp.float32), positions, q_count
    ).astype(jnp.bfloat16)
    new_keys = rotate_heads(
        jnp.dot(normed, k_weight, preferred_element_type=jnp.float32), positions, kv_count
    ).astype(jnp.bfloat16)
    new_vals = jnp.dot(normed, v_weight, preferred_element_type=jnp.float32).astype(jnp.bfloat16)
    all_keys = jnp.concatenate([cache_keys, new_keys], axis=0).reshape(
        slot_len + block_len, kv_count, HEAD
    )
    all_vals = jnp.concatenate([cache_vals, new_vals], axis=0).reshape(
        slot_len + block_len, kv_count, HEAD
    )
    grouped = queries.reshape(block_len, kv_count, q_count // kv_count, HEAD)
    scores = jnp.einsum(
        "bgid,kgd->gibk", grouped, all_keys, preferred_element_type=jnp.float32
    ) * HEAD ** (-0.5)
    valid = jnp.concatenate(
        [
            jnp.arange(slot_len, dtype=jnp.int32) < cache_length,
            jnp.ones((block_len,), dtype=jnp.bool_),
        ]
    )
    scores = jnp.where(valid, scores, -jnp.inf)
    peaks = jnp.max(scores, axis=-1, keepdims=True)
    expd = jnp.exp(scores - peaks)
    probs = (expd / jnp.sum(expd, axis=-1, keepdims=True)).astype(jnp.bfloat16)
    context = jnp.einsum("gibk,kgd->bgid", probs, all_vals, preferred_element_type=jnp.float32)
    context = context.astype(jnp.bfloat16).reshape(block_len, q_count * HEAD)
    return widened + jnp.dot(context, o_weight, preferred_element_type=jnp.float32)


def run_ffn(normed_rows, w_gate, w_up, w_down, down_all):
    part_rows = lax.all_gather(normed_rows, "blk", axis=0, tiled=True)
    gate_vals = jnp.dot(part_rows, w_gate, preferred_element_type=jnp.float32)
    up_vals = jnp.dot(part_rows, w_up, preferred_element_type=jnp.float32)
    hidden_all = (jax.nn.silu(gate_vals) * up_vals).astype(jnp.bfloat16)
    hidden_own = lax.all_to_all(hidden_all, "blk", 0, 1, tiled=True)
    groups = w_down.shape[0]
    group_count = down_all.shape[0] // groups
    terms = jnp.einsum(
        "rgk,gkd->grd",
        hidden_own.reshape(hidden_own.shape[0], group_count, groups),
        down_all.reshape(group_count, groups, down_all.shape[1]),
        preferred_element_type=jnp.float32,
    ).astype(jnp.bfloat16)
    return jnp.sum(terms.astype(jnp.float32), axis=0)


def fetch_slot(cache_kv, holder):
    count = lax.axis_size("req")
    own = cache_kv[0]
    if count != 8:
        slots = lax.all_gather(own, "req", axis=0, tiled=False)
        return slots[holder[0]]
    me = lax.axis_index("req")

    def swap(values, mask):
        return lax.ppermute(values, "req", perm=[(i, i ^ mask) for i in range(count)])

    def pick(cond, a, b):
        return jnp.where(cond, a, b)

    near = swap(holder, 1)
    quad = swap(jnp.concatenate([holder, near]), 2)
    holders = {0: holder[0], 1: near[0], 2: quad[0], 3: quad[1]}
    got1 = swap(own, 4)
    send_a = pick(holders[2] == me ^ 4, got1, own)
    send_b = pick(holders[3] == me ^ 4, got1, own)
    got2 = swap(jnp.stack([send_a, send_b]), 2)
    want = holders[1]
    send_c = pick(want == me, own, pick(want == me ^ 4, got1, got2[1]))
    got3 = swap(send_c, 1)
    need = holders[0]
    return pick(
        need == me,
        own,
        pick(
            need == me ^ 4, got1, pick(need ^ me == 2, got2[0], pick(need ^ me == 6, got2[0], got3))
        ),
    )


def local(
    tokens,
    cache_kv,
    cache_len,
    holder,
    accept,
    attn_gain,
    q_weight,
    k_weight,
    v_weight,
    o_weight,
    ffn_gain,
    w_gate,
    w_up,
    w_down,
):
    fetched = fetch_slot(cache_kv, holder)
    copies = jnp.broadcast_to(w_down[None], (lax.axis_size("blk"),) + w_down.shape)
    down_all = lax.all_to_all(copies, "blk", 0, 0, tiled=True).reshape(-1, w_down.shape[1])
    fetched, down_all = lax.optimization_barrier((fetched, down_all))
    cache_keys = fetched[0]
    cache_vals = fetched[1]
    cache_length = cache_len[0]
    block_rows = tokens[0]
    first_pass = attend_block(
        block_rows,
        cache_keys,
        cache_vals,
        cache_length,
        attn_gain,
        q_weight,
        k_weight,
        v_weight,
        o_weight,
    )
    chosen_mask = accept[0] == 1
    ffn_sum = run_ffn(
        rms_scale(first_pass, ffn_gain).astype(jnp.bfloat16), w_gate, w_up, w_down, down_all
    )
    placed = first_pass + ffn_sum
    second_in = jnp.where(chosen_mask[:, None], placed, block_rows.astype(jnp.float32))
    refined = attend_block(
        second_in,
        cache_keys,
        cache_vals,
        cache_length,
        attn_gain,
        q_weight,
        k_weight,
        v_weight,
        o_weight,
    )
    return refined[None]


def solution(mesh):
    return jax.shard_map(
        local,
        mesh=mesh,
        in_specs=(
            P(("req", "blk"), None, None),
            P(("req", "blk"), None, None, None),
            P(("req", "blk")),
            P(("req", "blk")),
            P(("req", "blk"), None),
            P(),
            P(),
            P(),
            P(),
            P(),
            P(),
            P(None, "blk"),
            P(None, "blk"),
            P("blk", None),
        ),
        out_specs=P(("req", "blk"), None, None),
        check_vma=False,
    )
```

profile of v0, /device:TPU:1, one launch (start us, length us, event | category | flops | bytes accessed | tf_op | source)
XLA Modules:
  0.0 477.4 jit_solution(10398602093591844268)
XLA Ops:
  6.5 7.1 %broadcast_in_dim.20 = bf16[32,128,1536]{2,1,0:T(8,128)(2,1)} broadcast(bf16[128,1536]{1,0:T(8,128)(2,1)} %param.27), dimensions={1,2} | broadcast | bytes 12976128 | tf_op jit(solution)/shard_map/broadcast_in_dim | solution.py:151
  13.6 10.4 %all-to-all-start = ((bf16[32,128,1536]{2,1,0:T(8,128)(2,1)}), bf16[32,128,1536]{2,1,0:T(8,128)(2,1)}, u32[]{:S(2)}, u32[]{:S(2)}) async-start(bf16[32,128,1536]{2,1,0:T(8,128)(2,1)} %broadcast_in_dim.20), calls=%async_computation | async-start | bytes 25165824 | tf_op jit(solution)/shard_map/all_to_all | solution.py:152
  24.0 2.8 collective-permute-start
  26.9 4.2 collective-permute-start.1
  31.8 4.4 copy.29
  37.0 3.3 fusion.55
  40.8 200.4 %collective-permute-done.1 = s32[1]{0:T(128)} collective-permute-done((s32[1]{0:T(128)}, s32[1]{0:T(128)}, u32[]{:S(2)}, u32[]{:S(2)}) %collective-permute-start.1) | collective-permute-done | bytes 36 | tf_op jit(solution)/shard_map/ppermute | solution.py:109
  242.0 1.2 collective-permute-start.2
  243.2 1.6 collective-permute-done.2
  249.8 2.5 copy.28
  252.3 1.9 subtract_convert_fusion.1
  254.1 2.3 convolution_convert_fusion.4
  256.5 1.2 fusion.57
  259.0 6.3 %collective-permute-done.3 = bf16[2,2,256,384]{3,2,1,0:T(8,128)(2,1)} collective-permute-done((bf16[2,2,256,384]{3,2,1,0:T(8,128)(2,1)}, bf16[2,2,256,384]{3,2,1,0:T(8,128)(2,1)}, u32[]{:S(2)}, u32[]{:S(2)}) %collective-permute-start.3) | collective-permute-done | bytes 786464 | tf_op jit(solution)/shard_map/ppermute | solution.py:109
  265.3 1.8 fusion.28
  268.3 1.6 copy.26
  269.9 1.6 pad_maximum_fusion.5
  271.5 1.6 subtract_convert_fusion.3
  273.1 6.1 %collective-permute-done.4 = bf16[2,256,384]{2,1,0:T(8,128)(2,1)} collective-permute-done((bf16[2,256,384]{2,1,0:T(8,128)(2,1)}, bf16[2,256,384]{2,1,0:T(8,128)(2,1)}, u32[]{:S(2)}, u32[]{:S(2)}) %collective-permute-start.4) | collective-permute-done | bytes 393248 | tf_op jit(solution)/shard_map/ppermute | solution.py:109
  279.2 1.9 fusion.24
  281.1 34.0 %all-to-all-done = bf16[32,128,1536]{2,1,0:T(8,128)(2,1)} async-done(((bf16[32,128,1536]{2,1,0:T(8,128)(2,1)}), bf16[32,128,1536]{2,1,0:T(8,128)(2,1)}, u32[]{:S(2)}, u32[]{:S(2)}) %all-to-all-start) | async-done | bytes 12582944 | tf_op jit(solution)/shard_map/all_to_all | solution.py:152
  316.6 2.8 fusion.78
  319.4 1.7 convolution_convert_fusion.2
  323.6 78.8 %all-gather.2.cloned.1.call-done = bf16[4096,1536]{1,0:T(8,128)(2,1)} async-done(((bf16[128,1536]{1,0:T(8,128)(2,1)}), bf16[4096,1536]{1,0:T(8,128)(2,1)}) %all-gather.2.cloned.1.call-update) | async-done | bytes 12582928 | tf_op jit(solution)/shard_map/all_gather | solution.py:84
  402.4 8.0 %fusion.84 = f32[4096,128]{1,0:T(8,128)S(1)} fusion(bf16[4096,1536]{1,0:T(8,128)(2,1)} %all-gather.2.cloned.1.call-done, bf16[1536,128]{1,0:T(8,128)(2,1)S(1)} %copy-done.12), kind=kOutput, calls=%fused_computation.105 | convolution fusion | flops 1610612736 | bytes 15073280 | tf_op jit(solution)/shard_map/dot_general | solution.py:85
  410.6 4.6 fusion.2
  415.2 6.9 %all-to-all-start.1 = ((bf16[32,128,128]{2,1,0:T(8,128)(2,1)}), bf16[32,128,128]{2,1,0:T(8,128)(2,1)}, u32[]{:S(2)}, u32[]{:S(2)}) async-start(bf16[32,128,128]{2,1,0:T(8,128)(2,1)} %bitcast.158), calls=%async_computation.1 | async-start | bytes 2097152 | tf_op jit(solution)/shard_map/all_to_all | solution.py:88
  422.1 27.9 %all-to-all-done.1 = bf16[32,128,128]{2,1,0:T(8,128)(2,1)} async-done(((bf16[32,128,128]{2,1,0:T(8,128)(2,1)}), bf16[32,128,128]{2,1,0:T(8,128)(2,1)}, u32[]{:S(2)}, u32[]{:S(2)}) %all-to-all-start.1) | async-done | bytes 1048608 | tf_op jit(solution)/shard_map/all_to_all | solution.py:88
  450.0 8.4 %convert_reduce_fusion = f32[128,1536]{1,0:T(8,128)S(1)} fusion(bf16[32,128,1536]{2,1,0:T(8,128)(2,1)} %bitcast.32, bf16[32,128,128]{2,1,0:T(8,128)(2,1)} %all-to-all-done.1), kind=kOutput, calls=%fused_computation.2 | convolution fusion | flops 1629290496 | bytes 14417920 | tf_op jit(solution)/shard_map/rgk,gkd->grd/dot_general | solution.py:91
  464.6 2.9 fusion.81
  467.5 1.7 convolution_convert_fusion.1
  469.2 1.4 fusion.3
  (81 shorter events, 16.5 us)
Async XLA Ops:
  6.5 314.6 %copy-start = (bf16[768,1536]{1,0:T(8,128)(2,1)S(1)}, bf16[768,1536]{1,0:T(8,128)(2,1)}, u32[]{:S(2)}) copy-start(bf16[768,1536]{1,0:T(8,128)(2,1)} %param.23) | copy-start | bytes 7077892
  13.6 10.4 %copy-start.8 = (bf16[1,2,256,384]{3,2,1,0:T(8,128)(2,1)S(1)}, bf16[1,2,256,384]{3,2,1,0:T(8,128)(2,1)}, u32[]{:S(2)}) copy-start(bf16[1,2,256,384]{3,2,1,0:T(8,128)(2,1)} %param.15) | copy-start | bytes 1179652
  13.6 301.5 %all-to-all-start = ((bf16[32,128,1536]{2,1,0:T(8,128)(2,1)}), bf16[32,128,1536]{2,1,0:T(8,128)(2,1)}, u32[]{:S(2)}, u32[]{:S(2)}) async-start(bf16[32,128,1536]{2,1,0:T(8,128)(2,1)} %broadcast_in_dim.20), calls=%async_computation | async-start | bytes 25165824 | tf_op jit(solution)/shard_map/all_to_all | solution.py:152
  24.0 378.4 %all-gather.2.cloned.1.call-start = ((), (), s32[]{:S(2)}) async-start(), calls=%async_computation.2 | async-start | bytes 12976128 | tf_op jit(solution)/shard_map/all_gather | solution.py:84
  24.0 222.7 %collective-permute-start = (bf16[2,256,384]{2,1,0:T(8,128)(2,1)S(1)}, bf16[2,256,384]{2,1,0:T(8,128)(2,1)S(1)}, u32[]{:S(2)}, u32[]{:S(2)}) collective-permute-start(bf16[2,256,384]{2,1,0:T(8,128)(2,1)S(1)} %bitcast.156), channel_id=1, source_target_pairs={{0,128},{32,160},{64,192},{96,224},{128,0},{160,32},{192,64},{224,... | collective-permute-start | bytes 1179656 | tf_op jit(solution)/shard_map/ppermute | solution.py:109
  26.9 214.4 %collective-permute-start.1 = (s32[1]{0:T(128)}, s32[1]{0:T(128)}, u32[]{:S(2)}, u32[]{:S(2)}) collective-permute-start(s32[1]{0:T(128)} %param.17), channel_id=1, source_target_pairs={{0,32},{32,0},{64,96},{96,64},{128,160},{160,128},{192,224},{224,1... | collective-permute-start | bytes 20 | tf_op jit(solution)/shard_map/ppermute | solution.py:109
  31.8 5.0 %copy-start.2 = (bf16[1,128,1536]{2,1,0:T(8,128)(2,1)S(1)}, bf16[1,128,1536]{2,1,0:T(8,128)(2,1)}, u32[]{:S(2)}) copy-start(bf16[1,128,1536]{2,1,0:T(8,128)(2,1)} %param.14) | copy-start | bytes 1179652
  31.8 5.2 %copy-start.17 = (f32[1536]{0:T(1024)S(1)}, f32[1536]{0:T(1024)}, u32[]{:S(2)}) copy-start(f32[1536]{0:T(1024)} %param.19) | copy-start | bytes 18436
  242.0 2.8 collective-permute-start.2
  246.7 2.3 copy-start.21
  247.8 17.5 %collective-permute-start.3 = (bf16[2,2,256,384]{3,2,1,0:T(8,128)(2,1)}, bf16[2,2,256,384]{3,2,1,0:T(8,128)(2,1)}, u32[]{:S(2)}, u32[]{:S(2)}) collective-permute-start(bf16[2,2,256,384]{3,2,1,0:T(8,128)(2,1)} %pad_maximum_fusion), channel_id=1, source_target_pairs={{0,64},{32,96},{64,0},{96,32},{128,192},{160,224},{192,128},{224,1... | collective-permute-start | bytes 2359304 | tf_op jit(solution)/shard_map/ppermute | solution.py:109
  252.3 4.2 copy-start.7
  267.1 12.1 %collective-permute-start.4 = (bf16[2,256,384]{2,1,0:T(8,128)(2,1)}, bf16[2,256,384]{2,1,0:T(8,128)(2,1)}, u32[]{:S(2)}, u32[]{:S(2)}) collective-permute-start(bf16[2,256,384]{2,1,0:T(8,128)(2,1)} %fusion.28), channel_id=1, source_target_pairs={{0,32},{32,0},{64,96},{96,64},{128,160},{160,128},{192,224},{224,1... | collective-permute-start | bytes 1179656 | tf_op jit(solution)/shard_map/ppermute | solution.py:109
  281.1 35.4 %copy-start.18 = (bf16[128,4,48]{0,2,1:T(8,128)(2,1)S(1)}, bf16[128,4,48]{0,2,1:T(8,128)(2,1)}, u32[]{:S(2)}) copy-start(bf16[128,4,48]{0,2,1:T(8,128)(2,1)} %get-tuple-element.21) | copy-start | bytes 147460
  281.1 35.4 %copy-start.19 = (bf16[128,4,48]{0,2,1:T(8,128)(2,1)S(1)}, bf16[128,4,48]{0,2,1:T(8,128)(2,1)}, u32[]{:S(2)}) copy-start(bf16[128,4,48]{0,2,1:T(8,128)(2,1)} %get-tuple-element.22) | copy-start | bytes 147460
  316.4 3.0 copy-start.15
  316.5 2.9 copy-start.13
  316.5 2.9 copy-start.16
  321.1 1.5 copy-start.20
  321.7 0.9 copy-start.4
  321.7 80.7 %copy-start.12 = (bf16[1536,128]{1,0:T(8,128)(2,1)S(1)}, bf16[1536,128]{1,0:T(8,128)(2,1)}, u32[]{:S(2)}) copy-start(bf16[1536,128]{1,0:T(8,128)(2,1)} %param.25) | copy-start | bytes 1179652
  323.5 86.8 %copy-start.22 = (bf16[1536,128]{1,0:T(8,128)(2,1)S(1)}, bf16[1536,128]{1,0:T(8,128)(2,1)}, u32[]{:S(2)}) copy-start(bf16[1536,128]{1,0:T(8,128)(2,1)} %param.26) | copy-start | bytes 1179652
  402.4 8.2 %copy-start.1 = (bf16[4096,1536]{1,0:T(8,128)(2,1)S(1)}, bf16[4096,1536]{1,0:T(8,128)(2,1)}, u32[]{:S(2)}) copy-start(bf16[4096,1536]{1,0:T(8,128)(2,1)} %all-gather.2.cloned.1.call-done) | copy-start | bytes 37748740
  415.2 6.9 %copy-start.23 = (s32[1,128]{1,0:T(1,128)S(1)}, s32[1,128]{1,0:T(1,128)}, u32[]{:S(2)}) copy-start(s32[1,128]{1,0:T(1,128)} %param.18) | copy-start | bytes 1540
  415.2 34.8 %all-to-all-start.1 = ((bf16[32,128,128]{2,1,0:T(8,128)(2,1)}), bf16[32,128,128]{2,1,0:T(8,128)(2,1)}, u32[]{:S(2)}, u32[]{:S(2)}) async-start(bf16[32,128,128]{2,1,0:T(8,128)(2,1)} %bitcast.158), calls=%async_computation.1 | async-start | bytes 2097152 | tf_op jit(solution)/shard_map/all_to_all | solution.py:88
  449.9 8.4 %copy-start.5 = (f32[128,1536]{1,0:T(8,128)S(1)}, f32[128,1536]{1,0:T(8,128)}, u32[]{:S(2)}) copy-start(f32[128,1536]{1,0:T(8,128)} %copy-done.4) | copy-start | bytes 2359300
  458.4 1.7 copy-start.3
  460.0 1.3 copy-start.6
  461.3 1.3 copy-start.9
  461.3 1.7 copy-start.10
  461.3 1.7 copy-start.11
  464.5 2.9 copy-start.14
Sparse Core Ops, SparseCore 0:
  323.7 78.6 all-gather.1
where the time goes:
time: 478 us; the launch traced here: 477 us
  waiting for transfers between devices  355 us (74%)
  matrix products  40.9 us (9%)
  starting transfers between devices  28 us (6%)
  local copies, waits for them, and re-layouts  20.8 us (4%)
  between operations  17.6 us (4%)
  other arithmetic  14.9 us (3%)
    ppermute x5, waiting for transfers between devices, swap(): lax.ppermute(values, 'req', perm=[(i, i ^ mask) for i in range(count)])  214 us
    all_gather x1, waiting for transfers between devices, run_ffn(): part_rows = lax.all_gather(normed_rows, 'blk', axis=0, tiled=True)  78.8 us
    all_to_all x1, waiting for transfers between devices, local(): lax.all_to_all(copies, 'blk', 0, 0, tiled=True).reshape(-1, w_down.shape[1])  34 us
    all_to_all x1, waiting for transfers between devices, run_ffn(): hidden_own = lax.all_to_all(hidden_all, 'blk', 0, 1, tiled=True)  27.9 us
    ppermute x5, starting transfers between devices, swap(): lax.ppermute(values, 'req', perm=[(i, i ^ mask) for i in range(count)])  10.7 us
    all_to_all x1, starting transfers between devices, local(): lax.all_to_all(copies, 'blk', 0, 0, tiled=True).reshape(-1, w_down.shape[1])  10.4 us
    unnamed x50, local copies, waits for them, and re-layouts  9.99 us
  transfers between devices with their start and end apart: 8, of which 7 were waited for; matrix products, arithmetic and copies ran while one was open for 6% of the time, Pallas kernels for 0%

commit v1 on v0

--- a/solution.py
+++ b/solution.py
@@ -85,7 +85,10 @@
     gate_vals = jnp.dot(part_rows, w_gate, preferred_element_type=jnp.float32)
     up_vals = jnp.dot(part_rows, w_up, preferred_element_type=jnp.float32)
     hidden_all = (jax.nn.silu(gate_vals) * up_vals).astype(jnp.bfloat16)
-    hidden_own = lax.all_to_all(hidden_all, "blk", 0, 1, tiled=True)
+    hidden_own = jnp.concatenate(
+        lax.all_to_all(jnp.stack(jnp.split(hidden_all, lax.axis_size("blk"), axis=0)), "blk", 0, 0),
+        axis=1,
+    )
     groups = w_down.shape[0]
     group_count = down_all.shape[0] // groups
     terms = jnp.einsum(

time: 478 us -> 494 us (1.033)
  local copies, waits for them, and re-layouts: 20.8 us -> 40.4 us
    unnamed x50 -> x85, local copies, waits for them, and re-layouts: 9.99 us -> 29 us
where the time goes in v1:
time: 494 us
  waiting for transfers between devices  355 us (72%)
  local copies, waits for them, and re-layouts  40.4 us (8%)
  matrix products  38.9 us (8%)
  starting transfers between devices  27.8 us (6%)
  between operations  17.5 us (4%)
  other arithmetic  13.5 us (3%)
    ppermute x5, waiting for transfers between devices, swap(): lax.ppermute(values, 'req', perm=[(i, i ^ mask) for i in range(count)])  214 us
    all_gather x1, waiting for transfers between devices, run_ffn(): part_rows = lax.all_gather(normed_rows, 'blk', axis=0, tiled=True)  78.8 us
    all_to_all x1, waiting for transfers between devices, local(): lax.all_to_all(copies, 'blk', 0, 0, tiled=True).reshape(-1, w_down.shape[1])  34.1 us
    unnamed x85, local copies, waits for them, and re-layouts  29 us
    all_to_all x1, waiting for transfers between devices, run_ffn(): lax.all_to_all(jnp.stack(jnp.split(hidden_all, lax.axis_size('blk'), axis...  27.9 us
    ppermute x5, starting transfers between devices, swap(): lax.ppermute(values, 'req', perm=[(i, i ^ mask) for i in range(count)])  10.7 us
    all_to_all x1, starting transfers between devices, local(): lax.all_to_all(copies, 'blk', 0, 0, tiled=True).reshape(-1, w_down.shape[1])  10.4 us
  transfers between devices with their start and end apart: 8, of which 7 were waited for; matrix products, arithmetic and copies ran while one was open for 6% of the time, Pallas kernels for 0%

profile of v1, /device:TPU:1, one launch (start us, length us, event | category | flops | bytes accessed | tf_op | source)
XLA Modules:
  0.0 493.5 jit_solution(16154002641867106493)
XLA Ops:
  6.5 7.1 %broadcast_in_dim.20 = bf16[32,128,1536]{2,1,0:T(8,128)(2,1)} broadcast(bf16[128,1536]{1,0:T(8,128)(2,1)} %param.27), dimensions={1,2} | broadcast | bytes 12976128 | tf_op jit(solution)/shard_map/broadcast_in_dim | solution.py:154
  13.6 10.4 %all-to-all-start = ((bf16[32,128,1536]{2,1,0:T(8,128)(2,1)}), bf16[32,128,1536]{2,1,0:T(8,128)(2,1)}, u32[]{:S(2)}, u32[]{:S(2)}) async-start(bf16[32,128,1536]{2,1,0:T(8,128)(2,1)} %broadcast_in_dim.20), calls=%async_computation | async-start | bytes 25165824 | tf_op jit(solution)/shard_map/all_to_all | solution.py:155
  24.1 2.8 collective-permute-start
  26.9 4.2 collective-permute-start.1
  31.8 4.3 copy.29
  37.0 3.3 fusion.55
  40.8 200.5 %collective-permute-done.1 = s32[1]{0:T(128)} collective-permute-done((s32[1]{0:T(128)}, s32[1]{0:T(128)}, u32[]{:S(2)}, u32[]{:S(2)}) %collective-permute-start.1) | collective-permute-done | bytes 36 | tf_op jit(solution)/shard_map/ppermute | solution.py:112
  241.9 1.2 collective-permute-start.2
  243.1 1.6 collective-permute-done.2
  249.7 2.5 copy.28
  252.2 1.9 subtract_convert_fusion.1
  254.1 2.3 convolution_convert_fusion.4
  256.4 1.2 fusion.57
  258.7 6.4 %collective-permute-done.3 = bf16[2,2,256,384]{3,2,1,0:T(8,128)(2,1)} collective-permute-done((bf16[2,2,256,384]{3,2,1,0:T(8,128)(2,1)}, bf16[2,2,256,384]{3,2,1,0:T(8,128)(2,1)}, u32[]{:S(2)}, u32[]{:S(2)}) %collective-permute-start.3) | collective-permute-done | bytes 786464 | tf_op jit(solution)/shard_map/ppermute | solution.py:112
  265.2 1.8 fusion.28
  268.1 1.6 copy.26
  269.8 1.7 pad_maximum_fusion.5
  271.4 1.6 subtract_convert_fusion.3
  273.1 6.0 %collective-permute-done.4 = bf16[2,256,384]{2,1,0:T(8,128)(2,1)} collective-permute-done((bf16[2,256,384]{2,1,0:T(8,128)(2,1)}, bf16[2,256,384]{2,1,0:T(8,128)(2,1)}, u32[]{:S(2)}, u32[]{:S(2)}) %collective-permute-start.4) | collective-permute-done | bytes 393248 | tf_op jit(solution)/shard_map/ppermute | solution.py:112
  279.1 1.9 fusion.24
  281.0 34.1 %all-to-all-done = bf16[32,128,1536]{2,1,0:T(8,128)(2,1)} async-done(((bf16[32,128,1536]{2,1,0:T(8,128)(2,1)}), bf16[32,128,1536]{2,1,0:T(8,128)(2,1)}, u32[]{:S(2)}, u32[]{:S(2)}) %all-to-all-start) | async-done | bytes 12582944 | tf_op jit(solution)/shard_map/all_to_all | solution.py:155
  316.6 2.8 fusion.78
  319.4 1.7 convolution_convert_fusion.2
  322.8 78.8 %all-gather.2.cloned.1.call-done = bf16[4096,1536]{1,0:T(8,128)(2,1)} async-done(((bf16[128,1536]{1,0:T(8,128)(2,1)}), bf16[4096,1536]{1,0:T(8,128)(2,1)}) %all-gather.2.cloned.1.call-update) | async-done | bytes 12582928 | tf_op jit(solution)/shard_map/all_gather | solution.py:84
  401.6 8.0 %fusion.84 = f32[4096,128]{1,0:T(8,128)S(1)} fusion(bf16[4096,1536]{1,0:T(8,128)(2,1)} %all-gather.2.cloned.1.call-done, bf16[1536,128]{1,0:T(8,128)(2,1)} %param.25), kind=kOutput, calls=%fused_computation.169 | convolution fusion | flops 1610612736 | bytes 15073280 | tf_op jit(solution)/shard_map/dot_general | solution.py:85
  409.9 3.7 fusion.2
  433.2 6.7 %all-to-all-start.1 = ((bf16[32,128,128]{2,1,0:T(8,128)(2,1)}), bf16[32,128,128]{2,1,0:T(8,128)(2,1)}, u32[]{:S(2)}, u32[]{:S(2)}) async-start(bf16[32,128,128]{2,1,0:T(8,128)(2,1)} %constant_dynamic-update-slice_fusion), calls=%async_computation.1 | async-start | bytes 2097152 | tf_op jit(solution)/shard_map/all_to_all | solution.py:89
  440.0 27.9 %all-to-all-done.1 = bf16[32,128,128]{2,1,0:T(8,128)(2,1)} async-done(((bf16[32,128,128]{2,1,0:T(8,128)(2,1)}), bf16[32,128,128]{2,1,0:T(8,128)(2,1)}, u32[]{:S(2)}, u32[]{:S(2)}) %all-to-all-start.1) | async-done | bytes 1048608 | tf_op jit(solution)/shard_map/all_to_all | solution.py:89
  467.9 8.3 %convert_reduce_fusion = f32[128,1536]{1,0:T(8,128)S(1)} fusion(bf16[32,128,1536]{2,1,0:T(8,128)(2,1)} %bitcast.63, bf16[32,128,128]{2,1,0:T(8,128)(2,1)} %all-to-all-done.1), kind=kOutput, calls=%fused_computation.2 | convolution fusion | flops 1629290496 | bytes 14417920 | tf_op jit(solution)/shard_map/rgk,gkd->grd/dot_general | solution.py:94
  481.7 1.8 fusion.81
  483.5 1.8 convolution_convert_fusion.1
  485.3 1.4 fusion.3
  (117 shorter events, 34.6 us)
Async XLA Ops:
  6.5 314.6 %copy-start = (bf16[768,1536]{1,0:T(8,128)(2,1)S(1)}, bf16[768,1536]{1,0:T(8,128)(2,1)}, u32[]{:S(2)}) copy-start(bf16[768,1536]{1,0:T(8,128)(2,1)} %param.23) | copy-start | bytes 7077892
  13.6 10.4 %copy-start.8 = (bf16[1,2,256,384]{3,2,1,0:T(8,128)(2,1)S(1)}, bf16[1,2,256,384]{3,2,1,0:T(8,128)(2,1)}, u32[]{:S(2)}) copy-start(bf16[1,2,256,384]{3,2,1,0:T(8,128)(2,1)} %param.15) | copy-start | bytes 1179652
  13.6 301.5 %all-to-all-start = ((bf16[32,128,1536]{2,1,0:T(8,128)(2,1)}), bf16[32,128,1536]{2,1,0:T(8,128)(2,1)}, u32[]{:S(2)}, u32[]{:S(2)}) async-start(bf16[32,128,1536]{2,1,0:T(8,128)(2,1)} %broadcast_in_dim.20), calls=%async_computation | async-start | bytes 25165824 | tf_op jit(solution)/shard_map/all_to_all | solution.py:155
  24.0 377.6 %all-gather.2.cloned.1.call-start = ((), (), s32[]{:S(2)}) async-start(), calls=%async_computation.2 | async-start | bytes 12976128 | tf_op jit(solution)/shard_map/all_gather | solution.py:84
  24.1 222.6 %collective-permute-start = (bf16[2,256,384]{2,1,0:T(8,128)(2,1)S(1)}, bf16[2,256,384]{2,1,0:T(8,128)(2,1)S(1)}, u32[]{:S(2)}, u32[]{:S(2)}) collective-permute-start(bf16[2,256,384]{2,1,0:T(8,128)(2,1)S(1)} %bitcast.283), channel_id=1, source_target_pairs={{0,128},{32,160},{64,192},{96,224},{128,0},{160,32},{192,64},{224,... | collective-permute-start | bytes 1179656 | tf_op jit(solution)/shard_map/ppermute | solution.py:112
  26.9 214.4 %collective-permute-start.1 = (s32[1]{0:T(128)}, s32[1]{0:T(128)}, u32[]{:S(2)}, u32[]{:S(2)}) collective-permute-start(s32[1]{0:T(128)} %param.17), channel_id=1, source_target_pairs={{0,32},{32,0},{64,96},{96,64},{128,160},{160,128},{192,224},{224,1... | collective-permute-start | bytes 20 | tf_op jit(solution)/shard_map/ppermute | solution.py:112
  31.8 5.0 %copy-start.2 = (bf16[1,128,1536]{2,1,0:T(8,128)(2,1)S(1)}, bf16[1,128,1536]{2,1,0:T(8,128)(2,1)}, u32[]{:S(2)}) copy-start(bf16[1,128,1536]{2,1,0:T(8,128)(2,1)} %param.14) | copy-start | bytes 1179652
  31.8 5.2 %copy-start.17 = (f32[1536]{0:T(1024)S(1)}, f32[1536]{0:T(1024)}, u32[]{:S(2)}) copy-start(f32[1536]{0:T(1024)} %param.19) | copy-start | bytes 18436
  241.9 2.8 collective-permute-start.2
  246.6 2.3 copy-start.21
  247.7 17.5 %collective-permute-start.3 = (bf16[2,2,256,384]{3,2,1,0:T(8,128)(2,1)}, bf16[2,2,256,384]{3,2,1,0:T(8,128)(2,1)}, u32[]{:S(2)}, u32[]{:S(2)}) collective-permute-start(bf16[2,2,256,384]{3,2,1,0:T(8,128)(2,1)} %pad_maximum_fusion), channel_id=1, source_target_pairs={{0,64},{32,96},{64,0},{96,32},{128,192},{160,224},{192,128},{224,1... | collective-permute-start | bytes 2359304 | tf_op jit(solution)/shard_map/ppermute | solution.py:112
  252.2 4.2 copy-start.7
  267.0 12.1 %collective-permute-start.4 = (bf16[2,256,384]{2,1,0:T(8,128)(2,1)}, bf16[2,256,384]{2,1,0:T(8,128)(2,1)}, u32[]{:S(2)}, u32[]{:S(2)}) collective-permute-start(bf16[2,256,384]{2,1,0:T(8,128)(2,1)} %fusion.28), channel_id=1, source_target_pairs={{0,32},{32,0},{64,96},{96,64},{128,160},{160,128},{192,224},{224,1... | collective-permute-start | bytes 1179656 | tf_op jit(solution)/shard_map/ppermute | solution.py:112
  269.8 46.8 %copy-start.24 = (pred[384]{0:T(512)(128)(4,1)}, pred[384]{0:T(512)(128)(4,1)S(1)}, u32[]{:S(2)}) copy-start(pred[384]{0:T(512)(128)(4,1)S(1)} %concatenate.51) | copy-start | bytes 1156
  281.0 35.6 %copy-start.18 = (bf16[128,4,48]{0,2,1:T(8,128)(2,1)S(1)}, bf16[128,4,48]{0,2,1:T(8,128)(2,1)}, u32[]{:S(2)}) copy-start(bf16[128,4,48]{0,2,1:T(8,128)(2,1)} %get-tuple-element.21) | copy-start | bytes 147460
  281.0 35.6 %copy-start.19 = (bf16[128,4,48]{0,2,1:T(8,128)(2,1)S(1)}, bf16[128,4,48]{0,2,1:T(8,128)(2,1)}, u32[]{:S(2)}) copy-start(bf16[128,4,48]{0,2,1:T(8,128)(2,1)} %get-tuple-element.22) | copy-start | bytes 147460
  316.4 3.0 copy-start.14
  316.5 2.9 copy-start.12
  316.6 2.9 copy-start.16
  401.6 8.3 %copy-start.1 = (bf16[4096,1536]{1,0:T(8,128)(2,1)S(1)}, bf16[4096,1536]{1,0:T(8,128)(2,1)}, u32[]{:S(2)}) copy-start(bf16[4096,1536]{1,0:T(8,128)(2,1)} %all-gather.2.cloned.1.call-done) | copy-start | bytes 37748740
  401.6 8.3 %copy-start.22 = (bf16[1536,128]{1,0:T(8,128)(2,1)S(1)}, bf16[1536,128]{1,0:T(8,128)(2,1)}, u32[]{:S(2)}) copy-start(bf16[1536,128]{1,0:T(8,128)(2,1)} %param.26) | copy-start | bytes 1179652
  423.4 16.6 %copy-start.23 = (s32[1,128]{1,0:T(1,128)S(1)}, s32[1,128]{1,0:T(1,128)}, u32[]{:S(2)}) copy-start(s32[1,128]{1,0:T(1,128)} %param.18) | copy-start | bytes 1540
  433.2 34.7 %all-to-all-start.1 = ((bf16[32,128,128]{2,1,0:T(8,128)(2,1)}), bf16[32,128,128]{2,1,0:T(8,128)(2,1)}, u32[]{:S(2)}, u32[]{:S(2)}) async-start(bf16[32,128,128]{2,1,0:T(8,128)(2,1)} %constant_dynamic-update-slice_fusion), calls=%async_computation.1 | async-start | bytes 2097152 | tf_op jit(solution)/shard_map/all_to_all | solution.py:89
  476.2 2.0 copy-start.3
  478.2 1.3 copy-start.6
  479.5 1.3 copy-start.9
  479.5 1.7 copy-start.10
  479.5 1.7 copy-start.11
  480.7 0.9 copy-start.15
  480.7 0.9 copy-start.25
  481.7 1.8 copy-start.13
  483.5 1.8 copy-start.5
  (2 other events, 1.6 us)
Sparse Core Ops, SparseCore 0:
  322.9 78.6 all-gather.1
